TPU v7x, 512 devices: a whole 4x4x16 slice. The times are simulated.
512 devices in a mesh: expert: 32 (over y, z_hi, x), dp: 16 (over z_lo, core).
Axes of the slice: x: 4, y: 4, z: 16 (z_hi: 2, z_lo: 8; z = z_hi * 8 + z_lo), core: 2. Of those that a mesh axis runs over, the one named last changes fastest.
Arguments:
- tokens: bfloat16 [4096, 3584], P('expert'), may hold values from -6 to 6
- expert_ids: int32 [4096, 8], P('expert'), may hold values from 0 to 31, all different within a row; in each aligned block of 128 rows (0 to 127, 128 to 255, ...) at most 48 rows name the same one
- route_weights: float32 [4096, 8], P('expert'), may hold values from 0.05 to 0.45
- gate_up_panels: bfloat16 [32, 16, 1792, 256], P('expert', 'dp'), may hold values from -0.09375 to 0.09375
- down_panels: bfloat16 [32, 1024, 3584], P('expert', None, 'dp'), may hold values from -0.1875 to 0.1875
- partner: int32 [32], replicated, may hold values from 0 to 31, as said below
Outputs:
- moe_out: bfloat16 [4096, 3584], P('expert', 'dp')
- new_gate_up: bfloat16 [32, 16, 1792, 256], P('expert', 'dp')
- new_down: bfloat16 [32, 1024, 3584], P('expert', None, 'dp')
Inputs may be any that keep to these rules, and one draw needn't show every extreme that they name: `expert_ids`: in the 128 rows of one index of the expert axis, each row names 8 different experts and no expert is named by more than 48 rows. partner[i] is i, i XOR 1 or i XOR 2, the same of these for the four indices of each aligned group of four; partner[partner[i]] = i; some group takes XOR 1 and some group XOR 2.
All inputs are finite; a program needn't handle non-finite values.
Results may differ from a plain program's by a relative error of at most 0.0057.
Values may be sent and summed in bfloat16 or wider, within the bound.
No kernel may reach another device: no remote copies, remote signals or barrier semaphores. Data moves between devices by JAX's collectives and lax.ppermute only.
A program may use at most 64 MiB of HBM per device.

v0:
```python
import jax
import jax.numpy as jnp
from jax import lax
from jax.sharding import PartitionSpec as P


def from_partner(block, axis, bit):
    count = lax.axis_size(axis)
    route = []
    for low in range(count):
        high = low | 1 << bit
        if high != low and high < count:
            route += [(low, high), (high, low)]
    return lax.ppermute(block, axis, route)


def swap_panels(gate_up, down, partner):
    here = lax.axis_index("expert")
    partner_id = partner[here]
    result_gate_up, result_down = (gate_up, down)
    for bit_number in range(2):
        moved_gate_up, moved_down = from_partner((gate_up, down), "expert", bit_number)
        taken = partner_id == jnp.bitwise_xor(here, 1 << bit_number)
        result_gate_up = jnp.where(taken, moved_gate_up, result_gate_up)
        result_down = jnp.where(taken, moved_down, result_down)
    return (result_gate_up, result_down)


def run_layer(tokens, expert_ids, route_weights, gate_up, down, owner_table):
    devices = lax.axis_size("expert")
    token_rows, model_width = tokens.shape
    top_count = expert_ids.shape[1]
    expert_count = owner_table.shape[0]
    capacity = min(token_rows, 3 * token_rows * top_count // (2 * expert_count))
    half_width = model_width // 2
    side = lax.rem(lax.axis_index("dp"), 2)
    own_half = lax.dynamic_slice_in_dim(tokens, side * half_width, half_width, 1)
    labels = jnp.arange(expert_count, dtype=jnp.int32)
    onehot = (expert_ids[:, :, None] == labels[None, None, :]).astype(jnp.int32)
    picked = jnp.sum(onehot, axis=1)
    slot_rank = jnp.cumsum(picked, axis=0) - picked
    slots = jnp.sum(onehot * slot_rank[:, None, :], axis=2)
    target = jnp.sum(onehot * owner_table[None, None, :], axis=2)
    place = (target * capacity + slots).reshape(-1)
    row_ids = jnp.repeat(jnp.arange(token_rows, dtype=jnp.int32), top_count)
    source = jnp.full((devices * capacity,), token_rows, jnp.int32).at[place].set(row_ids)
    padded = jnp.concatenate([own_half, jnp.zeros((1, half_width), own_half.dtype)], axis=0)
    outgoing = padded[source].reshape(devices, capacity, half_width)
    arrived = lax.all_to_all(outgoing, "expert", split_axis=0, concat_axis=0, tiled=True)
    flat = arrived.reshape(devices * capacity, half_width)
    partial_value = jnp.dot(flat, gate_up, preferred_element_type=jnp.float32)
    half_rows = flat.shape[0] // 2
    mine = lax.dynamic_slice_in_dim(partial_value, side * half_rows, half_rows, 0)
    other = lax.dynamic_slice_in_dim(partial_value, (1 - side) * half_rows, half_rows, 0)
    summed = mine + from_partner(other, "dp", 0)
    block_units = gate_up.shape[1] // 2
    hidden = (jax.nn.silu(summed[:, :block_units]) * summed[:, block_units:]).astype(jnp.bfloat16)
    gathered = lax.all_gather(hidden, "dp", axis=1, tiled=True)
    pair_count = lax.axis_size("dp") // 2
    out_columns = down.shape[1]
    outputs = jnp.einsum(
        "rqhk,qkc->hrc",
        gathered.reshape(half_rows, pair_count, 2, block_units),
        down.reshape(pair_count, block_units, out_columns),
        preferred_element_type=jnp.float32,
    )
    expert_out = outputs.reshape(devices, capacity, out_columns).astype(jnp.bfloat16)
    returned = lax.all_to_all(expert_out, "expert", split_axis=0, concat_axis=0, tiled=True)
    chosen = returned.reshape(devices * capacity, out_columns)[place].reshape(
        token_rows, top_count, out_columns
    )
    mixed = jnp.sum(chosen.astype(jnp.float32) * route_weights[:, :, None], axis=1)
    return mixed.astype(jnp.bfloat16)


def per_device(tokens, expert_ids, route_weights, gate_up_panels, down_panels, partner):
    new_gate_up, new_down = swap_panels(gate_up_panels, down_panels, partner)
    moe_out = run_layer(tokens, expert_ids, route_weights, new_gate_up[0, 0], new_down[0], partner)
    return (moe_out, new_gate_up, new_down)


def solution(mesh):
    return jax.shard_map(
        per_device,
        mesh=mesh,
        in_specs=(
            P("expert", None),
            P("expert", None),
            P("expert", None),
            P("expert", "dp", None, None),
            P("expert", None, "dp"),
            P(),
        ),
        out_specs=(P("expert", "dp"), P("expert", "dp", None, None), P("expert", None, "dp")),
        check_vma=False,
    )
```

profile of v0, /device:TPU:1, one launch (start us, length us, event | category | flops | bytes accessed | tf_op | source)
XLA Modules:
  0.0 459.5 jit_solution(5787766010149977916)
XLA Ops:
  7.2 0.0 copy-start
  7.2 0.8 convert_reduce_fusion
  8.0 0.1 copy.24
  8.1 0.2 reduce_window_sum.11
  8.3 0.1 copy.26
  8.3 0.8 select_reduce_fusion.1
  9.1 0.1 copy.27
  9.2 0.1 add.55
  9.4 0.1 reshape.99
  9.5 4.3 scatter_custom_fusion
  13.8 0.0 copy-done
  13.9 6.7 %gather_fusion = bf16[1536,1792]{1,0:T(8,128)(2,1)} fusion(bf16[129,1792]{1,0:T(8,128)(2,1)S(1)} %concatenate.3, s32[2048]{0:T(1024)S(1)} %pad_clamp_fusion), kind=kCustom, calls=%fused_computation | custom fusion | bytes 11016192 | tf_op jit(solution)/shard_map/gather | solution.py:48
  20.7 0.0 copy-start.2
  20.7 0.0 copy-start.6
  20.7 21.4 %all-to-all-start = ((bf16[32,48,1792]{2,1,0:T(8,128)(2,1)}), bf16[32,48,1792]{2,1,0:T(8,128)(2,1)}, u32[]{:S(2)}, u32[]{:S(2)}) async-start(bf16[32,48,1792]{2,1,0:T(8,128)(2,1)} %bitcast.31), calls=%async_computation | async-start | bytes 11010048 | tf_op jit(solution)/shard_map/all_to_all | solution.py:49
  42.0 0.0 all-gather.2.cloned.1.call-start
  42.1 0.0 copy-done.2
  42.1 4.6 collective-permute-start.2
  46.7 2.2 collective-permute-start.3
  48.9 0.0 copy-done.6
  48.9 0.6 dynamic_slice.12
  50.8 80.2 %collective-permute-done.2 = bf16[1,1,1792,256]{3,2,1,0:T(8,128)(2,1)S(1)} collective-permute-done((bf16[1,1,1792,256]{3,2,1,0:T(8,128)(2,1)S(1)}, bf16[1,1,1792,256]{3,2,1,0:T(8,128)(2,1)S(1)}, u32[]{:S(2)}, u32[]{:S(2)}) %collective-permute-start.2) | collective-permute-done | bytes 917536 | tf_op jit(solution)/shard_map/ppermute | solution.py:14
  131.0 0.0 copy-start.4
  131.0 0.9 copy-done.4
  131.9 24.1 %collective-permute-done.3 = bf16[1,1,1792,256]{3,2,1,0:T(8,128)(2,1)} collective-permute-done((bf16[1,1,1792,256]{3,2,1,0:T(8,128)(2,1)S(1)}, bf16[1,1,1792,256]{3,2,1,0:T(8,128)(2,1)}, u32[]{:S(2)}, u32[]{:S(2)}) %collective-permute-start.3) | collective-permute-done | bytes 917536 | tf_op jit(solution)/shard_map/ppermute | solution.py:14
  156.0 1.3 select_select_fusion
  157.3 0.0 copy-start.3
  157.3 0.0 all-to-all-done
  157.3 4.5 fusion.12
  161.8 0.0 copy-done.3
  161.8 0.9 constant_dynamic-slice_fusion
  162.8 4.1 collective-permute-start.4
  166.9 2.1 collective-permute-done.4
  169.0 0.1 dynamic-slice_add_fusion
  169.1 0.8 fusion.16
  169.9 0.0 all-gather.2.cloned.1.call-update
  169.9 40.5 %collective-permute-start = (bf16[1,1024,224]{1,2,0:T(8,128)(2,1)}, bf16[1,1024,224]{1,2,0:T(8,128)(2,1)S(1)}, u32[]{:S(2)}, u32[]{:S(2)}) collective-permute-start(bf16[1,1024,224]{1,2,0:T(8,128)(2,1)} %param.10), channel_id=1, source_target_pairs={{0,32},{32,0},{16,48},{48,16},{64,96},{96,64},{80,112},{112,80},{1... | collective-permute-start | bytes 1376264 | tf_op jit(solution)/shard_map/ppermute | solution.py:14
  210.4 1.9 collective-permute-start.1
  212.3 8.8 %collective-permute-done = bf16[1,1024,224]{1,2,0:T(8,128)(2,1)S(1)} collective-permute-done((bf16[1,1024,224]{1,2,0:T(8,128)(2,1)}, bf16[1,1024,224]{1,2,0:T(8,128)(2,1)S(1)}, u32[]{:S(2)}, u32[]{:S(2)}) %collective-permute-start) | collective-permute-done | bytes 458784 | tf_op jit(solution)/shard_map/ppermute | solution.py:14
  221.1 8.9 %collective-permute-done.1 = bf16[1,1024,224]{1,2,0:T(8,128)(2,1)S(1)} collective-permute-done((bf16[1,1024,224]{1,2,0:T(8,128)(2,1)}, bf16[1,1024,224]{1,2,0:T(8,128)(2,1)S(1)}, u32[]{:S(2)}, u32[]{:S(2)}) %collective-permute-start.1) | collective-permute-done | bytes 458784 | tf_op jit(solution)/shard_map/ppermute | solution.py:14
  230.0 1.1 select_select_fusion.1
  231.1 0.0 copy-start.1
  231.1 0.1 copy.34
  231.2 157.7 %all-gather.2.cloned.1.call-done = bf16[768,2048]{1,0:T(8,128)(2,1)} async-done(((bf16[768,128]{1,0:T(8,128)(2,1)}), bf16[768,2048]{1,0:T(8,128)(2,1)}) %all-gather.2.cloned.1.call-update) | async-done | bytes 3145744 | tf_op jit(solution)/shard_map/all_gather | solution.py:58
  388.9 6.0 %reshape.76 = bf16[768,8,2,128]{3,2,1,0:T(2,128)(2,1)} reshape(bf16[768,2048]{1,0:T(8,128)(2,1)} %all-gather.2.cloned.1.call-done) | data formatting | bytes 6291456 | tf_op jit(solution)/shard_map/reshape | solution.py:63
  394.9 0.0 copy-done.1
  394.9 0.0 copy-start.5
  394.9 3.2 fusion.8
  398.1 1.2 copy.30
  399.3 10.9 %all-to-all-start.1 = ((bf16[32,48,224]{2,1,0:T(8,128)(2,1)}), bf16[32,48,224]{2,1,0:T(8,128)(2,1)S(1)}, u32[]{:S(2)}, u32[]{:S(2)}) async-start(bf16[32,48,224]{2,1,0:T(8,128)(2,1)} %bitcast.9), calls=%async_computation.1 | async-start | bytes 1572864 | tf_op jit(solution)/shard_map/all_to_all | solution.py:68
  410.2 0.0 copy-done.5
  410.2 0.1 copy.31
  410.3 37.3 %all-to-all-done.1 = bf16[32,48,224]{2,1,0:T(8,128)(2,1)S(1)} async-done(((bf16[32,48,224]{2,1,0:T(8,128)(2,1)}), bf16[32,48,224]{2,1,0:T(8,128)(2,1)S(1)}, u32[]{:S(2)}, u32[]{:S(2)}) %all-to-all-start.1) | async-done | bytes 688160 | tf_op jit(solution)/shard_map/all_to_all | solution.py:68
  447.6 3.9 gather_fusion.1
  451.6 0.4 fusion.11
  452.0 0.7 copy.32
  (9 shorter events, 0.1 us)
Async XLA Ops:
  7.2 6.7 %copy-start = (bf16[128,3584]{1,0:T(8,128)(2,1)S(1)}, bf16[128,3584]{1,0:T(8,128)(2,1)}, u32[]{:S(2)}) copy-start(bf16[128,3584]{1,0:T(8,128)(2,1)} %param.6) | copy-start | bytes 2752516
  20.7 21.4 %copy-start.2 = (bf16[1,1,1792,256]{3,2,1,0:T(8,128)(2,1)S(1)}, bf16[1,1,1792,256]{3,2,1,0:T(8,128)(2,1)}, u32[]{:S(2)}) copy-start(bf16[1,1,1792,256]{3,2,1,0:T(8,128)(2,1)} %param.9) | copy-start | bytes 2752516
  20.7 28.2 %copy-start.6 = (s32[32]{0:T(128)S(1)}, s32[32]{0:T(128)}, u32[]{:S(2)}) copy-start(s32[32]{0:T(128)} %param.11) | copy-start | bytes 388
  20.7 136.7 %all-to-all-start = ((bf16[32,48,1792]{2,1,0:T(8,128)(2,1)}), bf16[32,48,1792]{2,1,0:T(8,128)(2,1)}, u32[]{:S(2)}, u32[]{:S(2)}) async-start(bf16[32,48,1792]{2,1,0:T(8,128)(2,1)} %bitcast.31), calls=%async_computation | async-start | bytes 11010048 | tf_op jit(solution)/shard_map/all_to_all | solution.py:49
  42.0 346.9 %all-gather.2.cloned.1.call-start = ((), (), s32[]{:S(2)}) async-start(), calls=%async_computation.2 | async-start | bytes 3342336 | tf_op jit(solution)/shard_map/all_gather | solution.py:58
  42.1 88.9 %collective-permute-start.2 = (bf16[1,1,1792,256]{3,2,1,0:T(8,128)(2,1)S(1)}, bf16[1,1,1792,256]{3,2,1,0:T(8,128)(2,1)S(1)}, u32[]{:S(2)}, u32[]{:S(2)}) collective-permute-start(bf16[1,1,1792,256]{3,2,1,0:T(8,128)(2,1)S(1)} %copy-done.2), channel_id=1, source_target_pairs={{0,32},{32,0},{16,48},{48,16},{64,96},{96,64},{80,112},{112,80},{1... | collective-permute-start | bytes 2752520 | tf_op jit(solution)/shard_map/ppermute | solution.py:14
  46.7 109.3 %collective-permute-start.3 = (bf16[1,1,1792,256]{3,2,1,0:T(8,128)(2,1)S(1)}, bf16[1,1,1792,256]{3,2,1,0:T(8,128)(2,1)}, u32[]{:S(2)}, u32[]{:S(2)}) collective-permute-start(bf16[1,1,1792,256]{3,2,1,0:T(8,128)(2,1)S(1)} %copy-done.2), channel_id=1, source_target_pairs={{0,16},{16,0},{32,48},{48,32},{64,80},{80,64},{96,112},{112,96},{1... | collective-permute-start | bytes 2752520 | tf_op jit(solution)/shard_map/ppermute | solution.py:14
  131.0 0.9 copy-start.4
  157.3 4.5 copy-start.3
  162.8 6.2 %collective-permute-start.4 = (f32[768,256]{1,0:T(8,128)}, f32[768,256]{1,0:T(8,128)S(1)}, u32[]{:S(2)}, u32[]{:S(2)}) collective-permute-start(f32[768,256]{1,0:T(8,128)} %constant_dynamic-slice_fusion), channel_id=1, source_target_pairs={{0,1},{1,0},{2,3},{3,2},{4,5},{5,4},{6,7},{7,6},{8,9},{9,8},{10,11... | collective-permute-start | bytes 2359304 | tf_op jit(solution)/shard_map/ppermute | solution.py:14
  169.9 51.2 %collective-permute-start = (bf16[1,1024,224]{1,2,0:T(8,128)(2,1)}, bf16[1,1024,224]{1,2,0:T(8,128)(2,1)S(1)}, u32[]{:S(2)}, u32[]{:S(2)}) collective-permute-start(bf16[1,1024,224]{1,2,0:T(8,128)(2,1)} %param.10), channel_id=1, source_target_pairs={{0,32},{32,0},{16,48},{48,16},{64,96},{96,64},{80,112},{112,80},{1... | collective-permute-start | bytes 1376264 | tf_op jit(solution)/shard_map/ppermute | solution.py:14
  210.4 19.6 %collective-permute-start.1 = (bf16[1,1024,224]{1,2,0:T(8,128)(2,1)}, bf16[1,1024,224]{1,2,0:T(8,128)(2,1)S(1)}, u32[]{:S(2)}, u32[]{:S(2)}) collective-permute-start(bf16[1,1024,224]{1,2,0:T(8,128)(2,1)} %param.10), channel_id=1, source_target_pairs={{0,16},{16,0},{32,48},{48,32},{64,80},{80,64},{96,112},{112,96},{1... | collective-permute-start | bytes 1376264 | tf_op jit(solution)/shard_map/ppermute | solution.py:14
  231.1 163.8 %copy-start.1 = (bf16[1,1024,224]{1,2,0:T(8,128)(2,1)}, bf16[1,1024,224]{1,2,0:T(8,128)(2,1)S(1)}, u32[]{:S(2)}) copy-start(bf16[1,1024,224]{1,2,0:T(8,128)(2,1)S(1)} %select_select_fusion.1) | copy-start | bytes 1376260
  394.9 15.2 %copy-start.5 = (f32[128,8]{0,1:T(8,128)S(1)}, f32[128,8]{0,1:T(8,128)}, u32[]{:S(2)}) copy-start(f32[128,8]{0,1:T(8,128)} %param.8) | copy-start | bytes 12292
  399.3 48.3 %all-to-all-start.1 = ((bf16[32,48,224]{2,1,0:T(8,128)(2,1)}), bf16[32,48,224]{2,1,0:T(8,128)(2,1)S(1)}, u32[]{:S(2)}, u32[]{:S(2)}) async-start(bf16[32,48,224]{2,1,0:T(8,128)(2,1)} %bitcast.9), calls=%async_computation.1 | async-start | bytes 1572864 | tf_op jit(solution)/shard_map/all_to_all | solution.py:68
Sparse Core Ops, SparseCore 0:
  170.0 218.8 all-gather.1
where the time goes:
time: 460 us
  waiting for transfers between devices  319 us (69%)
  starting transfers between devices  85.5 us (19%)
  local copies, waits for them, and re-layouts  26.1 us (6%)
  between operations  15.6 us (3%)
  matrix products  7.64 us (2%)
  other arithmetic  5.51 us (1%)
    all_gather x1, waiting for transfers between devices, run_layer(): gathered = lax.all_gather(hidden, 'dp', axis=1, tiled=True)  158 us
    ppermute x5, waiting for transfers between devices, from_partner(): return lax.ppermute(block, axis, route)  124 us
    ppermute x5, starting transfers between devices, from_partner(): return lax.ppermute(block, axis, route)  53.3 us
    all_to_all x1, waiting for transfers between devices, run_layer(): lax.all_to_all(expert_out, 'expert', split_axis=0, concat_axis=0, tiled=T...  37.3 us
    all_to_all x1, starting transfers between devices, run_layer(): lax.all_to_all(outgoing, 'expert', split_axis=0, concat_axis=0, tiled=True)  21.4 us
    all_to_all x1, starting transfers between devices, run_layer(): lax.all_to_all(expert_out, 'expert', split_axis=0, concat_axis=0, tiled=T...  10.9 us
  transfers between devices with their start and end apart: 8, of which 7 were waited for; matrix products, arithmetic and copies ran while one was open for 1% of the time, Pallas kernels for 0%

commit v1 on v0

--- a/solution.py
+++ b/solution.py
@@ -55,7 +55,9 @@
     summed = mine + from_partner(other, "dp", 0)
     block_units = gate_up.shape[1] // 2
     hidden = (jax.nn.silu(summed[:, :block_units]) * summed[:, block_units:]).astype(jnp.bfloat16)
-    gathered = lax.all_gather(hidden, "dp", axis=1, tiled=True)
+    gathered = jnp.concatenate(
+        lax.all_to_all(jnp.stack([hidden] * lax.axis_size("dp")), "dp", 0, 0), axis=1
+    )
     pair_count = lax.axis_size("dp") // 2
     out_columns = down.shape[1]
     outputs = jnp.einsum(

time: 460 us -> 500 us (1.087)
  the two profiles are of different devices: /device:TPU:1 before, /device:TPU:482 now
where the time goes in v1:
time: 500 us; the launch traced here: 499 us
  waiting for transfers between devices  265 us (53%)
  starting transfers between devices  199 us (40%)
  local copies, waits for them, and re-layouts  22.4 us (4%)
  matrix products  7.49 us (1%)
    all_to_all x1, starting transfers between devices, run_layer(): lax.all_to_all(jnp.stack([hidden] * lax.axis_size('dp')), 'dp', 0, 0)  143 us
    ppermute x5, waiting for transfers between devices, from_partner(): return lax.ppermute(block, axis, route)  123 us
    all_to_all x1, waiting for transfers between devices, run_layer(): lax.all_to_all(jnp.stack([hidden] * lax.axis_size('dp')), 'dp', 0, 0)  109 us
    all_to_all x1, waiting for transfers between devices, run_layer(): lax.all_to_all(expert_out, 'expert', split_axis=0, concat_axis=0, tiled=T...  33.2 us
    all_to_all x1, starting transfers between devices, run_layer(): lax.all_to_all(expert_out, 'expert', split_axis=0, concat_axis=0, tiled=T...  23.4 us
    all_to_all x1, starting transfers between devices, run_layer(): lax.all_to_all(outgoing, 'expert', split_axis=0, concat_axis=0, tiled=True)  17.4 us
    ppermute x5, starting transfers between devices, from_partner(): return lax.ppermute(block, axis, route)  14.6 us
  transfers between devices with their start and end apart: 8, of which 7 were waited for; matrix products, arithmetic and copies ran while one was open for 0% of the time, Pallas kernels for 0%

profile of v1, /device:TPU:482, one launch (start us, length us, event | category | flops | bytes accessed | tf_op | source)
XLA Modules:
  0.0 499.1 jit_solution(1747829135669584273)
XLA Ops:
  0.6 0.0 copy-start
  0.7 0.8 convert_reduce_fusion
  1.4 0.1 copy.23
  1.5 0.2 reduce_window_sum.11
  1.7 0.1 copy.25
  1.8 0.8 select_reduce_fusion.1
  2.6 0.1 copy.26
  2.7 0.1 add.55
  2.8 0.1 reshape.101
  2.9 4.3 scatter_custom_fusion
  7.3 0.0 copy-done
  7.4 6.7 %gather_fusion = bf16[1536,1792]{1,0:T(8,128)(2,1)} fusion(bf16[129,1792]{1,0:T(8,128)(2,1)S(1)} %concatenate.3, s32[2048]{0:T(1024)S(1)} %pad_clamp_fusion), kind=kCustom, calls=%fused_computation | custom fusion | bytes 11016192 | tf_op jit(solution)/shard_map/gather | solution.py:48
  14.1 0.0 copy-start.2
  14.1 0.0 copy-start.7
  14.1 17.4 %all-to-all-start = ((bf16[32,48,1792]{2,1,0:T(8,128)(2,1)}), bf16[32,48,1792]{2,1,0:T(8,128)(2,1)}, u32[]{:S(2)}, u32[]{:S(2)}) async-start(bf16[32,48,1792]{2,1,0:T(8,128)(2,1)} %bitcast.39), calls=%async_computation | async-start | bytes 11010048 | tf_op jit(solution)/shard_map/all_to_all | solution.py:49
  31.6 0.0 copy-done.2
  31.6 4.0 collective-permute-start.2
  35.5 3.4 collective-permute-start.3
  38.9 0.0 copy-done.7
  38.9 0.6 dynamic_slice.12
  40.8 83.4 %collective-permute-done.2 = bf16[1,1,1792,256]{3,2,1,0:T(8,128)(2,1)S(1)} collective-permute-done((bf16[1,1,1792,256]{3,2,1,0:T(8,128)(2,1)S(1)}, bf16[1,1,1792,256]{3,2,1,0:T(8,128)(2,1)S(1)}, u32[]{:S(2)}, u32[]{:S(2)}) %collective-permute-start.2) | collective-permute-done | bytes 917536 | tf_op jit(solution)/shard_map/ppermute | solution.py:14
  124.3 0.0 copy-start.4
  124.3 0.9 copy-done.4
  125.2 18.6 %collective-permute-done.3 = bf16[1,1,1792,256]{3,2,1,0:T(8,128)(2,1)} collective-permute-done((bf16[1,1,1792,256]{3,2,1,0:T(8,128)(2,1)S(1)}, bf16[1,1,1792,256]{3,2,1,0:T(8,128)(2,1)}, u32[]{:S(2)}, u32[]{:S(2)}) %collective-permute-start.3) | collective-permute-done | bytes 917536 | tf_op jit(solution)/shard_map/ppermute | solution.py:14
  143.8 1.3 select_select_fusion
  145.1 0.0 copy-start.3
  145.1 0.0 all-to-all-done
  145.1 4.5 fusion.3
  149.6 0.0 copy-done.3
  149.6 0.9 constant_dynamic-slice_fusion
  150.5 1.9 collective-permute-start.4
  152.5 2.5 collective-permute-done.4
  154.9 0.1 dynamic-slice_add_fusion
  155.0 0.1 fusion.7
  155.2 2.3 stack.2
  157.4 0.0 copy-start.5
  157.4 143.2 %all-to-all-start.1 = ((bf16[16,768,128]{2,1,0:T(8,128)(2,1)}), bf16[16,768,128]{2,1,0:T(8,128)(2,1)}, u32[]{:S(2)}, u32[]{:S(2)}) async-start(bf16[16,768,128]{2,1,0:T(8,128)(2,1)} %stack.2), calls=%async_computation.1 | async-start | bytes 6291456 | tf_op jit(solution)/shard_map/all_to_all | solution.py:59
  300.6 0.0 copy-done.5
  300.6 1.9 collective-permute-start
  302.5 3.4 collective-permute-start.1
  306.0 11.4 %collective-permute-done = bf16[1,1024,224]{1,2,0:T(8,128)(2,1)S(1)} collective-permute-done((bf16[1,1024,224]{1,2,0:T(8,128)(2,1)S(1)}, bf16[1,1024,224]{1,2,0:T(8,128)(2,1)S(1)}, u32[]{:S(2)}, u32[]{:S(2)}) %collective-permute-start) | collective-permute-done | bytes 458784 | tf_op jit(solution)/shard_map/ppermute | solution.py:14
  317.4 7.0 %collective-permute-done.1 = bf16[1,1024,224]{1,2,0:T(8,128)(2,1)S(1)} collective-permute-done((bf16[1,1024,224]{1,2,0:T(8,128)(2,1)S(1)}, bf16[1,1024,224]{1,2,0:T(8,128)(2,1)S(1)}, u32[]{:S(2)}, u32[]{:S(2)}) %collective-permute-start.1) | collective-permute-done | bytes 458784 | tf_op jit(solution)/shard_map/ppermute | solution.py:14
  324.4 0.1 select_select_fusion.1
  324.4 0.0 copy-start.1
  324.4 0.1 copy.33
  324.5 108.6 %all-to-all-done.1 = bf16[16,768,128]{2,1,0:T(8,128)(2,1)} async-done(((bf16[16,768,128]{2,1,0:T(8,128)(2,1)}), bf16[16,768,128]{2,1,0:T(8,128)(2,1)}, u32[]{:S(2)}, u32[]{:S(2)}) %all-to-all-start.1) | async-done | bytes 3145760 | tf_op jit(solution)/shard_map/all_to_all | solution.py:59
  433.1 0.0 copy-start.6
  433.1 3.0 fusion.1
  436.1 1.2 copy.29
  437.3 0.0 copy-done.1
  437.3 23.4 %all-to-all-start.2 = ((bf16[32,48,224]{2,1,0:T(8,128)(2,1)}), bf16[32,48,224]{2,1,0:T(8,128)(2,1)S(1)}, u32[]{:S(2)}, u32[]{:S(2)}) async-start(bf16[32,48,224]{2,1,0:T(8,128)(2,1)} %bitcast.11), calls=%async_computation.2 | async-start | bytes 1572864 | tf_op jit(solution)/shard_map/all_to_all | solution.py:70
  460.7 0.0 copy-done.6
  460.7 0.1 copy.30
  460.8 33.2 %all-to-all-done.2 = bf16[32,48,224]{2,1,0:T(8,128)(2,1)S(1)} async-done(((bf16[32,48,224]{2,1,0:T(8,128)(2,1)}), bf16[32,48,224]{2,1,0:T(8,128)(2,1)S(1)}, u32[]{:S(2)}, u32[]{:S(2)}) %all-to-all-start.2) | async-done | bytes 688160 | tf_op jit(solution)/shard_map/all_to_all | solution.py:70
  494.0 3.9 gather_fusion.1
  497.9 0.4 fusion.2
  498.3 0.7 copy.31
  (9 shorter events, 0.1 us)
Async XLA Ops:
  0.6 6.7 %copy-start = (bf16[128,3584]{1,0:T(8,128)(2,1)S(1)}, bf16[128,3584]{1,0:T(8,128)(2,1)}, u32[]{:S(2)}) copy-start(bf16[128,3584]{1,0:T(8,128)(2,1)} %param.6) | copy-start | bytes 2752516
  14.1 17.4 %copy-start.2 = (bf16[1,1,1792,256]{3,2,1,0:T(8,128)(2,1)S(1)}, bf16[1,1,1792,256]{3,2,1,0:T(8,128)(2,1)}, u32[]{:S(2)}) copy-start(bf16[1,1,1792,256]{3,2,1,0:T(8,128)(2,1)} %param.9) | copy-start | bytes 2752516
  14.1 24.8 %copy-start.7 = (s32[32]{0:T(128)S(1)}, s32[32]{0:T(128)}, u32[]{:S(2)}) copy-start(s32[32]{0:T(128)} %param.11) | copy-start | bytes 388
  14.1 130.9 %all-to-all-start = ((bf16[32,48,1792]{2,1,0:T(8,128)(2,1)}), bf16[32,48,1792]{2,1,0:T(8,128)(2,1)}, u32[]{:S(2)}, u32[]{:S(2)}) async-start(bf16[32,48,1792]{2,1,0:T(8,128)(2,1)} %bitcast.39), calls=%async_computation | async-start | bytes 11010048 | tf_op jit(solution)/shard_map/all_to_all | solution.py:49
  31.6 92.7 %collective-permute-start.2 = (bf16[1,1,1792,256]{3,2,1,0:T(8,128)(2,1)S(1)}, bf16[1,1,1792,256]{3,2,1,0:T(8,128)(2,1)S(1)}, u32[]{:S(2)}, u32[]{:S(2)}) collective-permute-start(bf16[1,1,1792,256]{3,2,1,0:T(8,128)(2,1)S(1)} %copy-done.2), channel_id=1, source_target_pairs={{0,32},{32,0},{16,48},{48,16},{64,96},{96,64},{80,112},{112,80},{1... | collective-permute-start | bytes 2752520 | tf_op jit(solution)/shard_map/ppermute | solution.py:14
  35.5 108.2 %collective-permute-start.3 = (bf16[1,1,1792,256]{3,2,1,0:T(8,128)(2,1)S(1)}, bf16[1,1,1792,256]{3,2,1,0:T(8,128)(2,1)}, u32[]{:S(2)}, u32[]{:S(2)}) collective-permute-start(bf16[1,1,1792,256]{3,2,1,0:T(8,128)(2,1)S(1)} %copy-done.2), channel_id=1, source_target_pairs={{0,16},{16,0},{32,48},{48,32},{64,80},{80,64},{96,112},{112,96},{1... | collective-permute-start | bytes 2752520 | tf_op jit(solution)/shard_map/ppermute | solution.py:14
  124.3 0.9 copy-start.4
  145.1 4.5 copy-start.3
  150.5 4.4 collective-permute-start.4
  157.4 143.2 %copy-start.5 = (bf16[1,1024,224]{1,2,0:T(8,128)(2,1)S(1)}, bf16[1,1024,224]{1,2,0:T(8,128)(2,1)}, u32[]{:S(2)}) copy-start(bf16[1,1024,224]{1,2,0:T(8,128)(2,1)} %param.10) | copy-start | bytes 1376260
  157.4 275.7 %all-to-all-start.1 = ((bf16[16,768,128]{2,1,0:T(8,128)(2,1)}), bf16[16,768,128]{2,1,0:T(8,128)(2,1)}, u32[]{:S(2)}, u32[]{:S(2)}) async-start(bf16[16,768,128]{2,1,0:T(8,128)(2,1)} %stack.2), calls=%async_computation.1 | async-start | bytes 6291456 | tf_op jit(solution)/shard_map/all_to_all | solution.py:59
  300.6 16.8 %collective-permute-start = (bf16[1,1024,224]{1,2,0:T(8,128)(2,1)S(1)}, bf16[1,1024,224]{1,2,0:T(8,128)(2,1)S(1)}, u32[]{:S(2)}, u32[]{:S(2)}) collective-permute-start(bf16[1,1024,224]{1,2,0:T(8,128)(2,1)S(1)} %copy-done.5), channel_id=1, source_target_pairs={{0,32},{32,0},{16,48},{48,16},{64,96},{96,64},{80,112},{112,80},{1... | collective-permute-start | bytes 1376264 | tf_op jit(solution)/shard_map/ppermute | solution.py:14
  302.5 21.8 %collective-permute-start.1 = (bf16[1,1024,224]{1,2,0:T(8,128)(2,1)S(1)}, bf16[1,1024,224]{1,2,0:T(8,128)(2,1)S(1)}, u32[]{:S(2)}, u32[]{:S(2)}) collective-permute-start(bf16[1,1024,224]{1,2,0:T(8,128)(2,1)S(1)} %copy-done.5), channel_id=1, source_target_pairs={{0,16},{16,0},{32,48},{48,32},{64,80},{80,64},{96,112},{112,96},{1... | collective-permute-start | bytes 1376264 | tf_op jit(solution)/shard_map/ppermute | solution.py:14
  324.4 112.8 %copy-start.1 = (bf16[1,1024,224]{1,2,0:T(8,128)(2,1)}, bf16[1,1024,224]{1,2,0:T(8,128)(2,1)S(1)}, u32[]{:S(2)}) copy-start(bf16[1,1024,224]{1,2,0:T(8,128)(2,1)S(1)} %select_select_fusion.1) | copy-start | bytes 1376260
  433.1 27.6 %copy-start.6 = (f32[128,8]{0,1:T(8,128)S(1)}, f32[128,8]{0,1:T(8,128)}, u32[]{:S(2)}) copy-start(f32[128,8]{0,1:T(8,128)} %param.8) | copy-start | bytes 12292
  437.3 56.7 %all-to-all-start.2 = ((bf16[32,48,224]{2,1,0:T(8,128)(2,1)}), bf16[32,48,224]{2,1,0:T(8,128)(2,1)S(1)}, u32[]{:S(2)}, u32[]{:S(2)}) async-start(bf16[32,48,224]{2,1,0:T(8,128)(2,1)} %bitcast.11), calls=%async_computation.2 | async-start | bytes 1572864 | tf_op jit(solution)/shard_map/all_to_all | solution.py:70
